TPU v7x, 32 devices: a whole 2x2x4 slice. The times are simulated.
32 devices in a mesh: attn: 8 (over z, y), exp: 4 (over x, core).
Axes of the slice: x: 2, y: 2, z: 4, core: 2. Of those that a mesh axis runs over, the one named last changes fastest.
Arguments:
- q_latent: bfloat16 [16, 128, 512], P('attn'), may hold values from -6 to 6
- q_rope: bfloat16 [16, 64, 128], P('attn'), may hold values from -8 to 8
- cache_latent: bfloat16 [16, 4096, 512], P('attn', 'exp'), may hold values from -6 to 6
- cache_rope: bfloat16 [16, 64, 4096], P('attn', None, 'exp'), may hold values from -8 to 8
- lengths: int32 [16], P('attn'), may hold values from 2 to 4096, as said below
- tokens: bfloat16 [256, 7168], P(('attn', 'exp')), may hold values from -6 to 6
- route_ids: int32 [256, 4], P(('attn', 'exp')), may hold values from 0 to 7, all different within a row; in each aligned block of 8 rows (0 to 7, 8 to 15, ...) at most 8 rows name the same one
- route_gates: float32 [256, 4], P(('attn', 'exp')), may hold values from 0.2 to 1
- w_gate: bfloat16 [8, 7168, 1024], P('attn', None, 'exp'), may hold values from -0.0625 to 0.0625
- w_up: bfloat16 [8, 7168, 1024], P('attn', None, 'exp'), may hold values from -0.0625 to 0.0625
- w_down: bfloat16 [8, 1024, 7168], P('attn', 'exp'), may hold values from -0.1875 to 0.1875
Outputs:
- attn_out: bfloat16 [16, 128, 512], P('attn', 'exp')
- moe_out: bfloat16 [256, 7168], P(('attn', 'exp'))
Inputs may be any that keep to these rules, and one draw needn't show every extreme that they name: `route_ids`: within the rows of one device (aligned blocks of 8 rows) an expert is named at most 8 times; a token names 4 distinct experts. `lengths`: some request has length exactly 4096.
All inputs are finite; a program needn't handle non-finite values.
Results may differ from a plain program's by a relative error of at most 0.0058.
Values may be sent and summed in bfloat16 or wider, within the bound.
No kernel may reach another device: no remote copies, remote signals or barrier semaphores. Data moves between devices by JAX's collectives and lax.ppermute only.
A program may use at most 128 MiB of HBM per device.

v0:
```python
import math
import jax
import jax.numpy as jnp
from jax import lax
from jax.sharding import PartitionSpec as P

score_scale = 1.0 / math.sqrt(192.0)
neg_fill = -1e30


def expert_part(row_block, gate_slice, up_slice, down_slice):
    gate_value = jnp.dot(row_block, gate_slice, preferred_element_type=jnp.float32)
    upward = jnp.dot(row_block, up_slice, preferred_element_type=jnp.float32)
    hidden = (jax.nn.silu(gate_value) * upward).astype(jnp.bfloat16)
    return jnp.dot(hidden, down_slice, preferred_element_type=jnp.float32)


def per_device(
    q_latent,
    q_rope,
    cache_latent,
    cache_rope,
    lengths,
    tokens,
    route_ids,
    route_gates,
    w_gate,
    w_up,
    w_down,
):
    n_exp = lax.axis_size("exp")
    n_attn = lax.axis_size("attn")
    positions = cache_latent.shape[1]
    scores = jnp.einsum("rhl,rpl->rhp", q_latent, cache_latent, preferred_element_type=jnp.float32)
    scores = scores + jnp.einsum(
        "rdh,rdp->rhp", q_rope, cache_rope, preferred_element_type=jnp.float32
    )
    scores = score_scale * scores
    global_pos = lax.axis_index("exp") * positions + jnp.arange(positions, dtype=jnp.int32)
    is_live = global_pos[None, None, :] < lengths[:, None, None]
    masked = jnp.where(is_live, scores, neg_fill)
    block_max = jnp.max(masked, axis=2)
    weights = jnp.where(is_live, jnp.exp(masked - block_max[:, :, None]), 0.0)
    block_sum = jnp.sum(weights, axis=2)
    block_out = jnp.einsum(
        "rhp,rpl->rhl",
        weights.astype(jnp.bfloat16),
        cache_latent,
        preferred_element_type=jnp.float32,
    )
    row_top = lax.pmax(block_max, "exp")
    factor = jnp.exp(block_max - row_top)
    numerator, denominator = (
        lax.psum_scatter(block_out * factor[:, :, None], "exp", scatter_dimension=1, tiled=True),
        lax.psum_scatter(block_sum * factor, "exp", scatter_dimension=1, tiled=True),
    )
    attn_out = (numerator / denominator[:, :, None]).astype(jnp.bfloat16)
    n_local = w_gate.shape[0]
    all_axes = ("attn", "exp")
    tok_all = lax.all_gather(tokens, all_axes, axis=0, tiled=True)
    ids_all = lax.all_gather(route_ids, all_axes, axis=0, tiled=True)
    gates_all = lax.all_gather(route_gates, all_axes, axis=0, tiled=True)
    first_expert = lax.axis_index("attn") * n_local
    partial = None
    for i in range(n_local):
        weight = jnp.sum(jnp.where(ids_all == first_expert + i, gates_all, 0.0), axis=1)
        piece = expert_part(tok_all, w_gate[i], w_up[i], w_down[i]) * weight[:, None]
        partial = piece if partial is None else partial + piece
    moe_out = lax.psum_scatter(partial, all_axes, scatter_dimension=0, tiled=True).astype(
        jnp.bfloat16
    )
    return (attn_out, moe_out)


def solution(mesh):
    return jax.shard_map(
        per_device,
        mesh=mesh,
        in_specs=(
            P("attn", None, None),
            P("attn", None, None),
            P("attn", "exp", None),
            P("attn", None, "exp"),
            P("attn"),
            P(("attn", "exp"), None),
            P(("attn", "exp"), None),
            P(("attn", "exp"), None),
            P("attn", None, "exp"),
            P("attn", None, "exp"),
            P("attn", "exp", None),
        ),
        out_specs=(P("attn", "exp", None), P(("attn", "exp"), None)),
        check_vma=False,
    )
```

profile of v0, /device:TPU:0, one launch (start us, length us, event | category | flops | bytes accessed | tf_op | source)
XLA Modules:
  0.0 270.4 jit_solution(11026204819615197221)
XLA Ops:
  8.0 0.0 all-gather.4.cloned.1.call-start
  8.1 0.7 all-gather.4.cloned.1.call-update
  8.8 0.0 reduce-scatter.10.cloned.1.call-start
  8.8 0.7 broadcast_compare_fusion
  9.6 0.0 copy-done
  9.6 1.8 fusion.31
  11.4 1.2 fusion.30
  12.6 8.3 %pmax.7 = f32[2,128]{1,0:T(2,128)S(1)} all-reduce(f32[2,128]{1,0:T(2,128)S(1)} %get-tuple-element.4), channel_id=1, replica_groups=mesh['attn'=8,'exp'=4] {'exp'}, use_global_device_ids=true, to_apply=%region_1.2 | all-reduce | flops 256 | bytes 2048 | tf_op jit(solution)/shard_map/pmax | solution.py:51
  20.9 0.3 fusion.15
  21.3 0.7 copy.13
  22.0 0.0 reduce-scatter.6.cloned.1.call-start
  22.1 1.4 convolution_multiply_fusion.1
  23.5 0.0 reduce-scatter.8.cloned.1.call-start
  23.6 41.1 %all-gather = s32[32,8,4]{1,2,0:T(4,128)S(1)} all-gather(s32[1,8,4]{1,2,0:T(4,128)S(1)} %bitcast.28), channel_id=1, replica_groups=mesh['attn'=8,'exp'=4] {'attn','exp'}, dimensions={0}, use_global_device_ids=true | all-gather | bytes 4224 | tf_op jit(solution)/shard_map/all_gather | solution.py:61
  64.7 36.8 %all-gather.1 = f32[32,8,4]{1,2,0:T(4,128)S(1)} all-gather(f32[1,8,4]{1,2,0:T(4,128)S(1)} %bitcast.29), channel_id=1, replica_groups=mesh['attn'=8,'exp'=4] {'attn','exp'}, dimensions={0}, use_global_device_ids=true | all-gather | bytes 4224 | tf_op jit(solution)/shard_map/all_gather | solution.py:62
  101.5 0.1 select_reduce_fusion
  101.5 0.1 reshape.49
  101.6 4.3 %fusion.3 = f32[256,256]{1,0:T(8,128)S(1)} fusion(bf16[256,7168]{1,0:T(8,128)(2,1)} %all-gather.4.cloned.1.call-done, bf16[1,7168,256]{2,1,0:T(8,128)(2,1)} %param.19), kind=kOutput, calls=%fused_computation.4 | convolution fusion | flops 939524096 | bytes 7602176 | tf_op jit(solution)/shard_map/dot_general | solution.py:12
  105.9 11.2 %convolution_multiply_fusion = f32[256,7168]{1,0:T(8,128)} fusion(bf16[1,256,7168]{2,1,0:T(8,128)(2,1)} %param.21, f32[256]{0:T(256)S(1)} %reshape.49, bf16[256,7168]{1,0:T(8,128)(2,1)} %all-gather.4.cloned.1.call-done, bf16[1,7168,256]{2,1,0:T(8,128)(2,1)} %param.20, f32[256,256]{1,0:T(8,128)S(1)} %fusion.3), kind=kOutput, calls=%fused_computation | convolution fusion | flops 1881276416 | bytes 18613248 | tf_op jit(solution)/shard_map/dot_general | solution.py:15
  117.1 0.0 reduce-scatter.10.cloned.1.call-done
  117.1 0.8 copy.14
  117.9 1.6 divide_convert_fusion
  119.6 141.6 %reduce-scatter.8.cloned.1.call-done = f32[8,7168]{1,0:T(8,128)} async-done(((f32[256,7168]{1,0:T(8,128)}), f32[8,7168]{1,0:T(8,128)}) %reduce-scatter.8.cloned.1.call-update) | async-done | bytes 229392 | tf_op jit(solution)/shard_map/reduce_scatter | solution.py:69
  261.2 1.6 convert_element_type.15
  (14 shorter events, 0.1 us)
Async XLA Ops:
  8.0 1.6 copy-start
  8.0 3.3 %copy-start.1 = (bf16[2,64,1024]{2,1,0:T(8,128)(2,1)S(1)}, bf16[2,64,1024]{2,1,0:T(8,128)(2,1)}, u32[]{:S(2)}) copy-start(bf16[2,64,1024]{2,1,0:T(8,128)(2,1)} %param.14) | copy-start | bytes 786436
  8.0 93.6 %all-gather.4.cloned.1.call-start = ((), (), s32[]{:S(2)}) async-start(), calls=%async_computation.4 | async-start | bytes 3784704 | tf_op jit(solution)/shard_map/all_gather | solution.py:60
  8.8 108.4 %reduce-scatter.10.cloned.1.call-start = ((), (), s32[]{:S(2)}) async-start(), calls=%async_computation.6 | async-start | bytes 81920
  11.4 12.2 %copy-start.2 = (s32[8,4]{0,1:T(4,128)S(1)}, s32[8,4]{0,1:T(4,128)}, u32[]{:S(2)}) copy-start(s32[8,4]{0,1:T(4,128)} %param.17) | copy-start | bytes 388
  11.4 53.3 %copy-start.3 = (f32[8,4]{0,1:T(4,128)S(1)}, f32[8,4]{0,1:T(4,128)}, u32[]{:S(2)}) copy-start(f32[8,4]{0,1:T(4,128)} %param.18) | copy-start | bytes 388
  22.0 95.9 %reduce-scatter.6.cloned.1.call-start = ((), (), s32[]{:S(2)}) async-start(), calls=%async_computation.3 | async-start | bytes 655360 | tf_op jit(solution)/shard_map/reduce_scatter | solution.py:54
  23.5 237.7 %reduce-scatter.8.cloned.1.call-start = ((), (), s32[]{:S(2)}) async-start(), calls=%async_computation.5 | async-start | bytes 7569408 | tf_op jit(solution)/shard_map/reduce_scatter | solution.py:69
Sparse Core Ops, SparseCore 0:
  11.7 63.1 all-gather.3
Sparse Core Ops, SparseCore 1:
  22.1 19.7 reduce-scatter.9
  44.4 25.2 reduce-scatter.5
  117.2 144.0 reduce-scatter.7
where the time goes:
time: 271 us; the launch traced here: 270 us
  waiting for transfers between devices  142 us (52%)
  blocking collectives  86.2 us (32%)
  matrix products  19.8 us (7%)
  between operations  15.8 us (6%)
  other arithmetic  4.34 us (2%)
    reduce_scatter x1, waiting for transfers between devices, per_device(): lax.psum_scatter(partial, all_axes, scatter_dimension=0, tiled=True)  142 us
    all_gather x1, blocking collectives, per_device(): ids_all = lax.all_gather(route_ids, all_axes, axis=0, tiled=True)  41.1 us
    all_gather x1, blocking collectives, per_device(): gates_all = lax.all_gather(route_gates, all_axes, axis=0, tiled=True)  36.8 us
    dot_general x1, matrix products, expert_part(): return jnp.dot(hidden, down_slice, preferred_element_type=jnp.float32)  11.2 us
    pmax x1, blocking collectives, per_device(): row_top = lax.pmax(block_max, 'exp')  8.33 us
  transfers between devices with their start and end apart: 4, of which 1 were waited for; matrix products, arithmetic and copies ran while one was open for 9% of the time, Pallas kernels for 0%

commit v1 on v0

--- a/solution.py
+++ b/solution.py
@@ -58,8 +58,13 @@
     n_local = w_gate.shape[0]
     all_axes = ("attn", "exp")
     tok_all = lax.all_gather(tokens, all_axes, axis=0, tiled=True)
-    ids_all = lax.all_gather(route_ids, all_axes, axis=0, tiled=True)
-    gates_all = lax.all_gather(route_gates, all_axes, axis=0, tiled=True)
+    ids_all, gates_all = jnp.split(
+        lax.all_gather(
+            jnp.concatenate([route_ids, route_gates], axis=1), all_axes, axis=0, tiled=True
+        ),
+        [route_ids.shape[1]],
+        axis=1,
+    )
     first_expert = lax.axis_index("attn") * n_local
     partial = None
     for i in range(n_local):

time: 271 us -> 246 us (0.908)
  blocking collectives: 86.2 us -> 49.6 us
  waiting for transfers between devices: 142 us -> 154 us
    all_gather x2 -> x1, blocking collectives: 77.9 us -> 41.3 us  [per_device(): lax.all_gather(jnp.concatenate([route_ids, route_gates], axis=1), all_axe...]
    all_gather x1, waiting for transfers between devices: 0.02 us -> 9.63 us  [per_device(): tok_all = lax.all_gather(tokens, all_axes, axis=0, tiled=True)]
  transfers between devices with their start and end apart: 4 -> 4, of which waited for: 1 -> 2; matrix products, arithmetic and copies ran while one was open for 9% -> 10% of each run, Pallas kernels for 0% -> 0%
where the time goes in v1:
time: 246 us; the launch traced here: 245 us
  waiting for transfers between devices  154 us (63%)
  blocking collectives  49.6 us (20%)
  matrix products  19.8 us (8%)
  between operations  15.8 us (6%)
  other arithmetic  4.55 us (2%)
    reduce_scatter x1, waiting for transfers between devices, per_device(): lax.psum_scatter(partial, all_axes, scatter_dimension=0, tiled=True)  143 us
    all_gather x1, blocking collectives, per_device(): lax.all_gather(jnp.concatenate([route_ids, route_gates], axis=1), all_axe...  41.3 us
    dot_general x1, matrix products, expert_part(): return jnp.dot(hidden, down_slice, preferred_element_type=jnp.float32)  11.2 us
    all_gather x1, waiting for transfers between devices, per_device(): tok_all = lax.all_gather(tokens, all_axes, axis=0, tiled=True)  9.63 us
    pmax x1, blocking collectives, per_device(): row_top = lax.pmax(block_max, 'exp')  8.33 us
  transfers between devices with their start and end apart: 4, of which 2 were waited for; matrix products, arithmetic and copies ran while one was open for 10% of the time, Pallas kernels for 0%

profile of v1, /device:TPU:0, one launch (start us, length us, event | category | flops | bytes accessed | tf_op | source)
XLA Modules:
  0.0 245.1 jit_solution(15644179566429213008)
XLA Ops:
  8.0 0.0 all-gather.2.cloned.1.call-start
  8.1 0.7 all-gather.2.cloned.1.call-update
  8.8 0.0 reduce-scatter.10.cloned.1.call-start
  8.8 0.7 broadcast_compare_fusion
  9.6 1.8 fusion.32
  11.4 1.2 fusion.31
  12.6 8.3 %pmax.7 = f32[2,128]{1,0:T(2,128)S(1)} all-reduce(f32[2,128]{1,0:T(2,128)S(1)} %get-tuple-element.4), channel_id=1, replica_groups=mesh['attn'=8,'exp'=4] {'exp'}, use_global_device_ids=true, to_apply=%region_1.2 | all-reduce | flops 256 | bytes 2048 | tf_op jit(solution)/shard_map/pmax | solution.py:51
  20.9 0.3 fusion.15
  21.3 0.7 copy.15
  22.0 0.0 reduce-scatter.6.cloned.1.call-start
  22.1 1.4 convolution_multiply_fusion.1
  23.5 0.0 reduce-scatter.8.cloned.1.call-start
  23.6 0.1 copy.13
  23.6 0.1 copy.14
  23.7 0.1 pad_maximum_fusion
  23.8 41.3 %all_gather.7 = f32[256,8]{1,0:T(8,128)S(1)} all-gather(f32[8,8]{1,0:T(8,128)S(1)} %pad_maximum_fusion), channel_id=1, replica_groups=mesh['attn'=8,'exp'=4] {'attn','exp'}, dimensions={0}, use_global_device_ids=true | all-gather | bytes 8448 | tf_op jit(solution)/shard_map/all_gather | solution.py:62
  65.1 0.2 fusion.26
  65.3 9.6 %all-gather.2.cloned.1.call-done = bf16[256,7168]{1,0:T(8,128)(2,1)} async-done(((bf16[8,7168]{1,0:T(8,128)(2,1)}), bf16[256,7168]{1,0:T(8,128)(2,1)}) %all-gather.2.cloned.1.call-update) | async-done | bytes 3670032 | tf_op jit(solution)/shard_map/all_gather | solution.py:60
  74.9 4.3 %fusion.3 = f32[256,256]{1,0:T(8,128)S(1)} fusion(bf16[256,7168]{1,0:T(8,128)(2,1)} %all-gather.2.cloned.1.call-done, bf16[1,7168,256]{2,1,0:T(8,128)(2,1)} %param.19), kind=kOutput, calls=%fused_computation.4 | convolution fusion | flops 939524096 | bytes 7602176 | tf_op jit(solution)/shard_map/dot_general | solution.py:12
  79.2 11.2 %convolution_multiply_fusion = f32[256,7168]{1,0:T(8,128)} fusion(bf16[1,256,7168]{2,1,0:T(8,128)(2,1)} %param.21, f32[256]{0:T(256)S(1)} %fusion.26, bf16[256,7168]{1,0:T(8,128)(2,1)} %all-gather.2.cloned.1.call-done, bf16[1,7168,256]{2,1,0:T(8,128)(2,1)} %param.20, f32[256,256]{1,0:T(8,128)S(1)} %fusion.3), kind=kOutput, calls=%fused_computation | convolution fusion | flops 1881276416 | bytes 18613248 | tf_op jit(solution)/shard_map/dot_general | solution.py:15
  90.4 0.8 copy.16
  91.2 1.6 divide_convert_fusion
  92.8 143.1 %reduce-scatter.8.cloned.1.call-done = f32[8,7168]{1,0:T(8,128)} async-done(((f32[256,7168]{1,0:T(8,128)}), f32[8,7168]{1,0:T(8,128)}) %reduce-scatter.8.cloned.1.call-update) | async-done | bytes 229392 | tf_op jit(solution)/shard_map/reduce_scatter | solution.py:74
  236.0 1.6 convert_element_type.23
  (16 shorter events, 0.2 us)
Async XLA Ops:
  8.0 1.6 copy-start
  8.0 3.3 %copy-start.1 = (bf16[2,64,1024]{2,1,0:T(8,128)(2,1)S(1)}, bf16[2,64,1024]{2,1,0:T(8,128)(2,1)}, u32[]{:S(2)}) copy-start(bf16[2,64,1024]{2,1,0:T(8,128)(2,1)} %param.14) | copy-start | bytes 786436
  8.0 66.9 %all-gather.2.cloned.1.call-start = ((), (), s32[]{:S(2)}) async-start(), calls=%async_computation.4 | async-start | bytes 3784704 | tf_op jit(solution)/shard_map/all_gather | solution.py:60
  8.8 81.6 %reduce-scatter.10.cloned.1.call-start = ((), (), s32[]{:S(2)}) async-start(), calls=%async_computation.6 | async-start | bytes 81920
  11.4 12.2 %copy-start.2 = (s32[8,4]{0,1:T(4,128)S(1)}, s32[8,4]{0,1:T(4,128)}, u32[]{:S(2)}) copy-start(s32[8,4]{0,1:T(4,128)} %param.17) | copy-start | bytes 388
  11.4 12.3 %copy-start.3 = (f32[8,4]{0,1:T(4,128)S(1)}, f32[8,4]{0,1:T(4,128)}, u32[]{:S(2)}) copy-start(f32[8,4]{0,1:T(4,128)} %param.18) | copy-start | bytes 388
  22.0 69.2 %reduce-scatter.6.cloned.1.call-start = ((), (), s32[]{:S(2)}) async-start(), calls=%async_computation.3 | async-start | bytes 655360 | tf_op jit(solution)/shard_map/reduce_scatter | solution.py:54
  23.5 212.5 %reduce-scatter.8.cloned.1.call-start = ((), (), s32[]{:S(2)}) async-start(), calls=%async_computation.5 | async-start | bytes 7569408 | tf_op jit(solution)/shard_map/reduce_scatter | solution.py:74
Sparse Core Ops, SparseCore 0:
  11.7 63.1 all-gather.1
Sparse Core Ops, SparseCore 1:
  22.1 19.7 reduce-scatter.9
  44.4 25.2 reduce-scatter.5
  90.5 145.4 reduce-scatter.7
